TPU v7x, 256 devices: a whole 4x4x8 slice. The times are simulated.
256 devices in a mesh: fsdp: 16 (over z, core), batch: 16 (over y, x).
Axes of the slice: x: 4, y: 4, z: 8, core: 2. Of those that a mesh axis runs over, the one named last changes fastest.
Arguments:
- latents: bfloat16 [16, 16, 1024, 640], P('batch', 'fsdp'), may hold values from -6 to 6
- norm_gain: float32 [640], replicated, may hold values from 0.25 to 1.75
- second_gain: float32 [640], replicated, may hold values from 0.25 to 1.75
- spatial_w: bfloat16 [9, 640, 640], P(None, None, 'fsdp'), may hold values from -0.078125 to 0.078125
- temporal_w: bfloat16 [3, 640, 640], P(None, None, 'fsdp'), may hold values from -0.125 to 0.125
- critic_w: bfloat16 [16, 640, 640], P('batch'), may hold values from -0.25 to 0.25
- critic_head: float32 [16, 640], P('batch'), may hold values from -6 to 6
- targets: int32 [16, 32, 1], P('batch'), may hold values from 0 to 15; in each aligned block of 32 rows (0 to 31, 32 to 63, ..., all dimensions but the last counted through in order) at most 4 rows name the same one
- feasible: int32 [16, 16], P('batch', 'fsdp'), may hold values 0 or 1
Outputs:
- guided: bfloat16 [16, 16, 1024, 640], P('batch', 'fsdp')
Inputs may be any that keep to these rules, and one draw needn't show every extreme that they name: `targets`: among one candidate's 32 rows no critic group is named more than 4 times.
All inputs are finite; a program needn't handle non-finite values. No bound on the sum of `feasible` on one device may be relied on, other than what follows from the above.
Results may differ from a plain program's by a relative error of at most 0.0065.
Values may be sent and summed in bfloat16 or wider, within the bound.
No kernel may reach another device: no remote copies, remote signals or barrier semaphores. Data moves between devices by JAX's collectives and lax.ppermute only.
A program may use at most 128 MiB of HBM per device.

v0:
```python
import jax
import jax.numpy as jnp
import numpy as np
from jax import lax
from jax.sharding import Mesh
from jax.sharding import PartitionSpec as P

GROUPS = 32
IMG_ROWS = 32
IMG_COLS = 32
PIX = 1024
CAP = 4
FSDP = ("z", "c")
BATCH = ("y", "x")


def with_halo(array, axis, dim):
    size, length = (lax.axis_size(axis), array.shape[dim])
    up = [(i, (i + 1) % size) for i in range(size - 1)]
    down = [(j, i) for i, j in up]
    last = lax.slice_in_dim(array, length - 1, length, axis=dim)
    leading = lax.slice_in_dim(array, 0, 1, axis=dim)
    before = lax.ppermute(last, axis, up)
    after = lax.ppermute(leading, axis, down)
    return jnp.concatenate([before, array, after], axis=dim)


def group_silu(values, gain):
    shape = values.shape
    width = shape[-1]
    grouped = values.astype(jnp.float32).reshape(-1, shape[-2], GROUPS, width // GROUPS)
    center = jnp.mean(grouped, axis=(1, 3), keepdims=True)
    spread = jnp.mean((grouped - center) ** 2, axis=(1, 3), keepdims=True)
    normed = ((grouped - center) * lax.rsqrt(spread + 1e-05)).reshape(shape) * gain
    return jax.nn.silu(normed).astype(jnp.bfloat16)


def gather_out_major(weights):
    turned = jnp.swapaxes(weights, 1, 2)
    return lax.all_gather(turned, FSDP, axis=1, tiled=True)


def nt_dot(a, b):
    return lax.dot_general(a, b, (((1,), (1,)), ((), ())), preferred_element_type=jnp.float32)


def per_device(
    latents, norm_gain, second_gain, spatial_w, temporal_w, critic_w, critic_head, targets, feasible
):
    cands = latents.shape[0]
    width = latents.shape[-1]
    hid = critic_w.shape[-1]
    core = lax.axis_index("c")
    half = hid // 2
    own_half = lax.dynamic_slice_in_dim(critic_w[0], core * half, half, axis=1)
    mine = lax.all_gather(own_half, BATCH, axis=0, tiled=False)
    other = lax.ppermute(mine, "c", [(0, 1), (1, 0)])
    heads = lax.all_gather(critic_head[0], BATCH, axis=0, tiled=False)
    heads_mine = lax.dynamic_slice_in_dim(heads, core * half, half, axis=1)
    heads_other = lax.dynamic_slice_in_dim(heads, (1 - core) * half, half, axis=1)
    spatial_full = gather_out_major(spatial_w)
    temporal_full = gather_out_major(temporal_w)
    first = group_silu(latents, norm_gain)
    padded = jnp.pad(
        first.reshape(cands, IMG_ROWS, IMG_COLS, width), ((0, 0), (1, 1), (1, 1), (0, 0))
    )
    total = jnp.zeros((cands * PIX, spatial_full.shape[1]), jnp.float32)
    for offset in range(9):
        row_off, col_off = divmod(offset, 3)
        window = padded[:, row_off : row_off + IMG_ROWS, col_off : col_off + IMG_COLS].reshape(
            -1, width
        )
        total = total + nt_dot(window, spatial_full[offset])
    section = (latents.astype(jnp.float32) + total.reshape(latents.shape)).astype(jnp.bfloat16)
    second = group_silu(section, second_gain)
    beside_all = with_halo(second, FSDP, 1)
    total = jnp.zeros((cands * PIX, temporal_full.shape[1]), jnp.float32)
    for tap in range(3):
        total = total + nt_dot(beside_all[:, tap].reshape(-1, width), temporal_full[tap])
    denoised = (section.astype(jnp.float32) + total.reshape(latents.shape)).astype(jnp.bfloat16)
    groups = mine.shape[0]
    slots = cands * CAP
    flat_targets = targets.reshape(-1)
    chosen = (flat_targets[:, None] == jnp.arange(groups, dtype=jnp.int32)[None, :]).astype(
        jnp.int32
    )
    earlier = jnp.cumsum(chosen, axis=0) - chosen
    slot_of = jnp.sum(earlier * chosen, axis=1)
    live = jnp.repeat(feasible.reshape(-1), IMG_ROWS) > 0
    position = flat_targets * slots + slot_of
    placing = (
        (jnp.arange(groups * slots, dtype=jnp.int32)[:, None] == position[None, :]) & live[None, :]
    ).astype(jnp.bfloat16)
    rows = denoised.reshape(cands * IMG_ROWS, IMG_COLS * width)
    block = (
        jnp.dot(placing, rows, preferred_element_type=jnp.float32)
        .astype(jnp.bfloat16)
        .reshape(groups, slots * IMG_COLS, width)
    )

    def slope_of(w, h):
        pre = jnp.einsum("gtc,gch->gth", block, w, preferred_element_type=jnp.float32)
        return ((1.0 - jnp.tanh(pre) ** 2) * h[:, None, :]).astype(jnp.bfloat16)

    grads = jnp.einsum(
        "gth,gch->gtc", slope_of(mine, heads_mine), mine, preferred_element_type=jnp.float32
    ) + jnp.einsum(
        "gth,gch->gtc", slope_of(other, heads_other), other, preferred_element_type=jnp.float32
    )
    returned = grads.astype(jnp.bfloat16).reshape(groups * slots, -1)
    back = jnp.dot(placing.T, returned, preferred_element_type=jnp.float32)
    guided = (rows.astype(jnp.float32) - back).astype(jnp.bfloat16)
    return guided.reshape(latents.shape)


def solution(mesh):
    fine = Mesh(np.asarray(mesh.devices).reshape(8, 2, 4, 4), ("z", "c", "y", "x"))
    in_specs = (
        P(BATCH, FSDP, None, None),
        P(),
        P(),
        P(None, None, FSDP),
        P(None, None, FSDP),
        P(BATCH, None, None),
        P(BATCH, None),
        P(BATCH, None, None),
        P(BATCH, FSDP),
    )
    out_specs = P(BATCH, FSDP, None, None)
    return jax.shard_map(
        per_device, mesh=fine, in_specs=in_specs, out_specs=out_specs, check_vma=False
    )
```

profile of v0, /device:TPU:1, one launch (start us, length us, event | category | flops | bytes accessed | tf_op | source)
XLA Modules:
  0.0 253.1 jit_solution(7458203786415808206)
XLA Ops:
  6.5 1.1 copy-done
  7.7 0.2 constant_dynamic-slice_fusion.1
  7.9 1.0 copy.15
  9.0 0.7 all-gather.5.cloned.1.call-update
  9.7 0.7 all-gather.7.cloned.1.call-update
  10.4 0.2 convert_reduce_fusion.1
  10.8 0.1 reduce_sum.59
  11.1 0.4 fusion.13
  11.6 0.1 reduce_sum.62
  11.8 0.1 mul.100
  11.9 0.8 fusion.20
  12.7 5.3 %pad_slice_fusion = (bf16[1,32,32,640]{3,2,1,0:T(8,128)(2,1)}, bf16[1,32,32,640]{3,2,1,0:T(8,128)(2,1)}, bf16[1,32,32,640]{3,2,1,0:T(8,128)(2,1)}, bf16[1,32,32,...) fusion(bf16[1,32,32,640]{3,2,1,0:T(8,128)(2,1)S(1)} %bitcast.93), kind=kLoop, calls=%fused_computation.34 | loop fusion | bytes 11796480 | tf_op jit(solution)/shard_map/slice | solution.py:70
  18.0 62.9 %all-gather.9.cloned.1.call-done = bf16[16,640,320]{1,2,0:T(8,128)(2,1)} async-done(((bf16[1,640,320]{1,2,0:T(8,128)(2,1)}), bf16[16,640,320]{1,2,0:T(8,128)(2,1)}) %all-gather.9.cloned.1.call-update) | async-done | bytes 6553616 | tf_op jit(solution)/shard_map/all_gather | solution.py:56
  80.9 0.8 collective-permute-start.2
  81.8 52.3 %all-gather.5.cloned.1.call-done = bf16[9,640,640]{2,1,0:T(8,128)(2,1)} async-done(((bf16[9,40,640]{2,1,0:T(8,128)(2,1)}), bf16[9,640,640]{2,1,0:T(8,128)(2,1)}) %all-gather.5.cloned.1.call-update) | async-done | bytes 7372816 | tf_op jit(solution)/shard_map/all_gather | solution.py:40
  134.1 2.6 %fusion.32 = f32[1024,640]{1,0:T(8,128)S(1)} fusion(bf16[1,1,1024,640]{3,2,1,0:T(8,128)(2,1)S(1)} %fusion.20, bf16[9,640,640]{2,1,0:T(8,128)(2,1)} %all-gather.5.cloned.1.call-done), kind=kOutput, calls=%fused_computation.49 | convolution fusion | flops 838860800 | bytes 4751360 | tf_op jit(solution)/shard_map/dot_general | solution.py:44
  136.7 2.6 %fusion.36 = f32[1024,640]{1,0:T(8,128)S(1)} fusion(bf16[1024,640]{1,0:T(8,128)(2,1)S(1)} %bitcast.101, bf16[9,640,640]{2,1,0:T(8,128)(2,1)} %all-gather.5.cloned.1.call-done), kind=kOutput, calls=%fused_computation.58 | convolution fusion | flops 838860800 | bytes 4751360 | tf_op jit(solution)/shard_map/dot_general | solution.py:44
  139.3 2.6 %fusion.37 = f32[1024,640]{1,0:T(8,128)S(1)} fusion(bf16[1024,640]{1,0:T(8,128)(2,1)S(1)} %bitcast.100, bf16[9,640,640]{2,1,0:T(8,128)(2,1)} %all-gather.5.cloned.1.call-done), kind=kOutput, calls=%fused_computation.60 | convolution fusion | flops 838860800 | bytes 4751360 | tf_op jit(solution)/shard_map/dot_general | solution.py:44
  141.9 2.6 %fusion.38 = f32[1024,640]{1,0:T(8,128)S(1)} fusion(bf16[1024,640]{1,0:T(8,128)(2,1)S(1)} %bitcast.99, bf16[9,640,640]{2,1,0:T(8,128)(2,1)} %all-gather.5.cloned.1.call-done), kind=kOutput, calls=%fused_computation.62 | convolution fusion | flops 838860800 | bytes 4751360 | tf_op jit(solution)/shard_map/dot_general | solution.py:44
  144.5 2.7 %fusion.39 = f32[1024,640]{1,0:T(8,128)S(1)} fusion(bf16[1024,640]{1,0:T(8,128)(2,1)S(1)} %bitcast.98, bf16[9,640,640]{2,1,0:T(8,128)(2,1)} %all-gather.5.cloned.1.call-done), kind=kOutput, calls=%fused_computation.65 | convolution fusion | flops 838860800 | bytes 4751360 | tf_op jit(solution)/shard_map/dot_general | solution.py:44
  147.2 2.6 %fusion.40 = f32[1024,640]{1,0:T(8,128)S(1)} fusion(bf16[1024,640]{1,0:T(8,128)(2,1)S(1)} %bitcast.97, bf16[9,640,640]{2,1,0:T(8,128)(2,1)} %all-gather.5.cloned.1.call-done), kind=kOutput, calls=%fused_computation.67 | convolution fusion | flops 838860800 | bytes 4751360 | tf_op jit(solution)/shard_map/dot_general | solution.py:44
  149.8 2.6 %fusion.41 = f32[1024,640]{1,0:T(8,128)S(1)} fusion(bf16[1024,640]{1,0:T(8,128)(2,1)S(1)} %bitcast.96, bf16[9,640,640]{2,1,0:T(8,128)(2,1)} %all-gather.5.cloned.1.call-done), kind=kOutput, calls=%fused_computation.69 | convolution fusion | flops 838860800 | bytes 4751360 | tf_op jit(solution)/shard_map/dot_general | solution.py:44
  152.4 4.1 %fusion.42 = f32[1024,640]{1,0:T(8,128)} fusion(bf16[1024,640]{1,0:T(8,128)(2,1)S(1)} %bitcast.95, bf16[9,640,640]{2,1,0:T(8,128)(2,1)} %all-gather.5.cloned.1.call-done), kind=kOutput, calls=%fused_computation.71 | convolution fusion | flops 838860800 | bytes 4751360 | tf_op jit(solution)/shard_map/dot_general | solution.py:44
  156.5 3.8 %convert_reduce_fusion = (f32[640]{0:T(1024)S(1)}, bf16[1,1,1024,640]{3,2,1,0:T(8,128)(2,1)S(1)}) fusion(bf16[1024,640]{1,0:T(8,128)(2,1)S(1)} %bitcast.94, bf16[9,640,640]{2,1,0:T(8,128)(2,1)} %all-gather.5.cloned.1.call-done, f32[1024,640]{1,0:T(8,128)S(1)} %fusion.36, f32[1024,640]{1,0:T(8,128)S(1)} %fusion.37, f32[1024,640]{1,0:T(8,128)S(1)} %fusion.38, ...), kind=kOutput, calls=%fused_computation.6 | convolution fusion | flops 847379840 | bytes 25725440 | tf_op jit(solution)/shard_map/dot_general | solution.py:44
  160.4 0.1 reduce_sum.81
  160.6 0.1 sub.64
  160.7 0.4 fusion.5
  161.2 0.1 reduce_sum.84
  161.4 0.1 mul.107
  161.5 1.1 fusion.12
  162.6 1.9 collective-permute-start
  165.3 18.4 %all-gather = f32[16,1,640]{2,1,0:T(1,128)S(1)} all-gather(f32[1,1,640]{2,1,0:T(1,128)S(1)} %bitcast.104), channel_id=1, replica_groups=mesh['z'=8,'c'=2,'y'=4,'x'=4] {'y','x'}, dimensions={0}, use_global_device_ids=true | all-gather | bytes 43520 | tf_op jit(solution)/shard_map/all_gather | solution.py:58
  183.7 8.5 %collective-permute-start.1 = (bf16[1,1,1024,640]{3,2,1,0:T(8,128)(2,1)S(1)}, bf16[1,1,1024,640]{3,2,1,0:T(8,128)(2,1)}, u32[]{:S(2)}, u32[]{:S(2)}) collective-permute-start(bf16[1,1,1024,640]{3,2,1,0:T(8,128)(2,1)S(1)} %fusion.12), channel_id=1, source_target_pairs={{16,0},{32,16},{48,32},{64,48},{80,64},{96,80},{112,96},{128,112},... | collective-permute-start | bytes 3932168 | tf_op jit(solution)/shard_map/ppermute | solution.py:24
  192.3 0.2 constant_dynamic-slice_fusion.2
  192.4 0.2 select_reduce_fusion
  192.7 2.6 %fusion.28 = f32[1024,640]{1,0:T(8,128)S(1)} fusion(bf16[1,1,1024,640]{3,2,1,0:T(8,128)(2,1)S(1)} %fusion.12, bf16[3,640,640]{2,1,0:T(8,128)(2,1)} %all-gather.7.cloned.1.call-done), kind=kOutput, calls=%fused_computation.45 | convolution fusion | flops 838860800 | bytes 4751360 | tf_op jit(solution)/shard_map/dot_general | solution.py:44
  195.3 2.7 %fusion.30 = f32[1024,640]{1,0:T(8,128)S(1)} fusion(bf16[1,1,1024,640]{3,2,1,0:T(8,128)(2,1)} %collective-permute-done, bf16[3,640,640]{2,1,0:T(8,128)(2,1)S(1)} %copy-done.13), kind=kOutput, calls=%fused_computation.47 | convolution fusion | flops 838860800 | bytes 4751360 | tf_op jit(solution)/shard_map/dot_general | solution.py:44
  198.0 8.1 %collective-permute-done.1 = bf16[1,1,1024,640]{3,2,1,0:T(8,128)(2,1)} collective-permute-done((bf16[1,1,1024,640]{3,2,1,0:T(8,128)(2,1)S(1)}, bf16[1,1,1024,640]{3,2,1,0:T(8,128)(2,1)}, u32[]{:S(2)}, u32[]{:S(2)}) %collective-permute-start.1) | collective-permute-done | bytes 1310752 | tf_op jit(solution)/shard_map/ppermute | solution.py:24
  206.1 2.8 %fusion.22 = bf16[1,1,1024,640]{3,2,1,0:T(8,128)(2,1)S(1)} fusion(bf16[1,1,1024,640]{3,2,1,0:T(8,128)(2,1)S(1)} %get-tuple-element.16, f32[1024,640]{1,0:T(8,128)S(1)} %fusion.30, f32[1024,640]{1,0:T(8,128)S(1)} %fusion.28, bf16[1,1,1024,640]{3,2,1,0:T(8,128)(2,1)} %collective-permute-done.1, bf16[3,640,640]{2,1,0:T(8,128)(2,1)S(1)} %copy-done.13), kind=kOutput, calls=%fused_computation.31 | convolution fusion | flops 842137600 | bytes 9994240 | tf_op jit(solution)/shard_map/dot_general | solution.py:44
  209.0 0.6 reshape.217
  209.6 1.0 copy-done.3
  210.7 2.3 convolution_convert_fusion
  213.0 3.1 %reshape.219 = bf16[16,128,640]{2,1,0:T(8,128)(2,1)S(1)} reshape(bf16[64,20480]{1,0:T(8,128)(2,1)} %convolution_convert_fusion) | data formatting | bytes 5242880 | tf_op jit(solution)/shard_map/reshape | solution.py:98
  216.2 10.6 %fusion.23 = f32[16,128,640]{2,1,0:T(8,128)} fusion(bf16[16,640,320]{1,2,0:T(8,128)(2,1)} %all-gather.9.cloned.1.call-done, bf16[16,128,640]{2,1,0:T(8,128)(2,1)S(1)} %reshape.219, f32[16,320]{1,0:T(8,128)S(1)} %get-tuple-element.18), kind=kOutput, calls=%fused_computation.42 | convolution fusion | flops 1680343040 | bytes 14438400 | tf_op jit(solution)/shard_map/gth,gch->gtc/dot_general | solution.py:105
  226.8 11.3 %add_convert_fusion = bf16[16,128,640]{2,1,0:T(8,128)(2,1)} fusion(f32[16,128,640]{2,1,0:T(8,128)} %fusion.23, bf16[16,640,320]{1,2,0:T(8,128)(2,1)} %collective-permute-done.2, bf16[16,128,640]{2,1,0:T(8,128)(2,1)S(1)} %reshape.219, f32[16,320]{1,0:T(8,128)S(1)} %get-tuple-element.17), kind=kOutput, calls=%fused_computation.3 | convolution fusion | flops 1682964480 | bytes 17059840 | tf_op jit(solution)/shard_map/gth,gch->gtc/dot_general | solution.py:107
  238.1 4.6 %reshape.220 = bf16[64,20480]{1,0:T(8,128)(2,1)} reshape(bf16[16,128,640]{2,1,0:T(8,128)(2,1)} %add_convert_fusion) | data formatting | bytes 5242880 | tf_op jit(solution)/shard_map/reshape | solution.py:110
  242.7 2.4 fusion
  245.1 1.5 reshape.221
  (58 shorter events, 1.1 us)
Async XLA Ops:
  6.5 1.1 copy-start
  6.5 3.9 %copy-start.2 = (bf16[1,1,1024,640]{3,2,1,0:T(8,128)(2,1)S(1)}, bf16[1,1,1024,640]{3,2,1,0:T(8,128)(2,1)}, u32[]{:S(2)}) copy-start(bf16[1,1,1024,640]{3,2,1,0:T(8,128)(2,1)} %param.9) | copy-start | bytes 3932164
  6.5 74.4 %all-gather.9.cloned.1.call-start = ((), (), s32[]{:S(2)}) async-start(), calls=%async_computation.2 | async-start | bytes 6963200 | tf_op jit(solution)/shard_map/all_gather | solution.py:56
  7.7 4.2 %copy-start.14 = (f32[640]{0:T(1024)S(1)}, f32[640]{0:T(1024)}, u32[]{:S(2)}) copy-start(f32[640]{0:T(1024)} %param.10) | copy-start | bytes 7684
  8.9 125.2 %all-gather.5.cloned.1.call-start = ((), (), s32[]{:S(2)}) async-start(), calls=%async_computation | async-start | bytes 7833600 | tf_op jit(solution)/shard_map/all_gather | solution.py:40
  9.7 183.0 %all-gather.7.cloned.1.call-start = ((), (), s32[]{:S(2)}) async-start(), calls=%async_computation.1 | async-start | bytes 2611200 | tf_op jit(solution)/shard_map/all_gather | solution.py:40
  80.9 145.8 %collective-permute-start.2 = (bf16[16,640,320]{1,2,0:T(8,128)(2,1)}, bf16[16,640,320]{1,2,0:T(8,128)(2,1)}, u32[]{:S(2)}, u32[]{:S(2)}) collective-permute-start(bf16[16,640,320]{1,2,0:T(8,128)(2,1)} %all-gather.9.cloned.1.call-done), channel_id=1, source_target_pairs={{0,16},{16,0},{1,17},{17,1},{2,18},{18,2},{3,19},{19,3},{4,20},{20... | collective-permute-start | bytes 19660808 | tf_op jit(solution)/shard_map/ppermute | solution.py:57
  134.1 2.6 %copy-start.12 = (bf16[1,32,32,640]{3,2,1,0:T(8,128)(2,1)S(1)}, bf16[1,32,32,640]{3,2,1,0:T(8,128)(2,1)}, u32[]{:S(2)}) copy-start(bf16[1,32,32,640]{3,2,1,0:T(8,128)(2,1)} %get-tuple-element.11) | copy-start | bytes 3932164
  136.7 2.6 %copy-start.11 = (bf16[1,32,32,640]{3,2,1,0:T(8,128)(2,1)S(1)}, bf16[1,32,32,640]{3,2,1,0:T(8,128)(2,1)}, u32[]{:S(2)}) copy-start(bf16[1,32,32,640]{3,2,1,0:T(8,128)(2,1)} %get-tuple-element.10) | copy-start | bytes 3932164
  139.3 2.6 %copy-start.10 = (bf16[1,32,32,640]{3,2,1,0:T(8,128)(2,1)S(1)}, bf16[1,32,32,640]{3,2,1,0:T(8,128)(2,1)}, u32[]{:S(2)}) copy-start(bf16[1,32,32,640]{3,2,1,0:T(8,128)(2,1)} %get-tuple-element.9) | copy-start | bytes 3932164
  141.9 2.6 %copy-start.9 = (bf16[1,32,32,640]{3,2,1,0:T(8,128)(2,1)S(1)}, bf16[1,32,32,640]{3,2,1,0:T(8,128)(2,1)}, u32[]{:S(2)}) copy-start(bf16[1,32,32,640]{3,2,1,0:T(8,128)(2,1)} %get-tuple-element.8) | copy-start | bytes 3932164
  144.5 2.7 %copy-start.8 = (bf16[1,32,32,640]{3,2,1,0:T(8,128)(2,1)S(1)}, bf16[1,32,32,640]{3,2,1,0:T(8,128)(2,1)}, u32[]{:S(2)}) copy-start(bf16[1,32,32,640]{3,2,1,0:T(8,128)(2,1)} %get-tuple-element.7) | copy-start | bytes 3932164
  147.2 2.6 %copy-start.7 = (bf16[1,32,32,640]{3,2,1,0:T(8,128)(2,1)S(1)}, bf16[1,32,32,640]{3,2,1,0:T(8,128)(2,1)}, u32[]{:S(2)}) copy-start(bf16[1,32,32,640]{3,2,1,0:T(8,128)(2,1)} %get-tuple-element.6) | copy-start | bytes 3932164
  149.8 2.6 %copy-start.6 = (bf16[1,32,32,640]{3,2,1,0:T(8,128)(2,1)S(1)}, bf16[1,32,32,640]{3,2,1,0:T(8,128)(2,1)}, u32[]{:S(2)}) copy-start(bf16[1,32,32,640]{3,2,1,0:T(8,128)(2,1)} %get-tuple-element.12) | copy-start | bytes 3932164
  152.4 4.1 %copy-start.5 = (bf16[1,32,32,640]{3,2,1,0:T(8,128)(2,1)S(1)}, bf16[1,32,32,640]{3,2,1,0:T(8,128)(2,1)}, u32[]{:S(2)}) copy-start(bf16[1,32,32,640]{3,2,1,0:T(8,128)(2,1)} %get-tuple-element.5) | copy-start | bytes 3932164
  156.5 5.0 %copy-start.15 = (f32[640]{0:T(1024)S(1)}, f32[640]{0:T(1024)}, u32[]{:S(2)}) copy-start(f32[640]{0:T(1024)} %param.11) | copy-start | bytes 7684
  160.3 4.3 %copy-start.17 = (s32[1,32,1]{1,2,0:T(1,128)S(1)}, s32[1,32,1]{1,2,0:T(1,128)}, u32[]{:S(2)}) copy-start(s32[1,32,1]{1,2,0:T(1,128)} %param.16) | copy-start | bytes 388
  160.3 5.0 %copy-start.16 = (f32[1,640]{1,0:T(1,128)S(1)}, f32[1,640]{1,0:T(1,128)}, u32[]{:S(2)}) copy-start(f32[1,640]{1,0:T(1,128)} %param.15) | copy-start | bytes 7684
  162.6 32.7 %collective-permute-start = (bf16[1,1,1024,640]{3,2,1,0:T(8,128)(2,1)S(1)}, bf16[1,1,1024,640]{3,2,1,0:T(8,128)(2,1)}, u32[]{:S(2)}, u32[]{:S(2)}) collective-permute-start(bf16[1,1,1024,640]{3,2,1,0:T(8,128)(2,1)S(1)} %fusion.12), channel_id=1, source_target_pairs={{0,16},{16,32},{32,48},{48,64},{64,80},{80,96},{96,112},{112,128},... | collective-permute-start | bytes 3932168 | tf_op jit(solution)/shard_map/ppermute | solution.py:23
  183.7 22.4 %collective-permute-start.1 = (bf16[1,1,1024,640]{3,2,1,0:T(8,128)(2,1)S(1)}, bf16[1,1,1024,640]{3,2,1,0:T(8,128)(2,1)}, u32[]{:S(2)}, u32[]{:S(2)}) collective-permute-start(bf16[1,1,1024,640]{3,2,1,0:T(8,128)(2,1)S(1)} %fusion.12), channel_id=1, source_target_pairs={{16,0},{32,16},{48,32},{64,48},{80,64},{96,80},{112,96},{128,112},... | collective-permute-start | bytes 3932168 | tf_op jit(solution)/shard_map/ppermute | solution.py:24
  192.7 2.6 %copy-start.13 = (bf16[3,640,640]{2,1,0:T(8,128)(2,1)S(1)}, bf16[3,640,640]{2,1,0:T(8,128)(2,1)}, u32[]{:S(2)}) copy-start(bf16[3,640,640]{2,1,0:T(8,128)(2,1)} %all-gather.7.cloned.1.call-done) | copy-start | bytes 7372804
  209.6 1.1 copy-start.3
  238.1 4.6 %copy-start.4 = (bf16[32,20480]{1,0:T(8,128)(2,1)S(1)}, bf16[32,20480]{1,0:T(8,128)(2,1)}, u32[]{:S(2)}) copy-start(bf16[32,20480]{1,0:T(8,128)(2,1)} %copy-done.3) | copy-start | bytes 3932164
  242.7 3.9 %copy-start.1 = (bf16[1,640,640]{2,1,0:T(8,128)(2,1)S(1)}, bf16[1,640,640]{2,1,0:T(8,128)(2,1)}, u32[]{:S(2)}) copy-start(bf16[1,640,640]{2,1,0:T(8,128)(2,1)} %param.14) | copy-start | bytes 2457604
Sparse Core Ops, SparseCore 0:
  9.8 71.1 all-gather.8
  82.7 51.3 all-gather.4
  135.9 38.4 all-gather.6
where the time goes:
time: 254 us; the launch traced here: 253 us
  waiting for transfers between devices  125 us (49%)
  matrix products  60.7 us (24%)
  local copies, waits for them, and re-layouts  19.9 us (8%)
  blocking collectives  18.4 us (7%)
  between operations  14.2 us (6%)
  starting transfers between devices  11.4 us (4%)
  other arithmetic  3.74 us (1%)
    all_gather x1, waiting for transfers between devices, per_device(): mine = lax.all_gather(own_half, BATCH, axis=0, tiled=False)  62.9 us
    all_gather x2, waiting for transfers between devices, gather_out_major(): return lax.all_gather(turned, FSDP, axis=1, tiled=True)  52.4 us
    dot_general x12, matrix products, nt_dot(): lax.dot_general(a, b, (((1,), (1,)), ((), ())), preferred_element_type=jn...  34 us
    all_gather x1, blocking collectives, per_device(): heads = lax.all_gather(critic_head[0], BATCH, axis=0, tiled=False)  18.4 us
    dot_general x1, matrix products, per_device(): jnp.einsum('gth,gch->gtc', slope_of(other, heads_other), other, preferred...  11.3 us
    dot_general x1, matrix products, per_device(): jnp.einsum('gth,gch->gtc', slope_of(mine, heads_mine), mine, preferred_el...  10.6 us
    ppermute x1, starting transfers between devices, with_halo(): after = lax.ppermute(leading, axis, down)  8.55 us
    ppermute x1, waiting for transfers between devices, with_halo(): after = lax.ppermute(leading, axis, down)  8.15 us
  transfers between devices with their start and end apart: 6, of which 3 were waited for; matrix products, arithmetic and copies ran while one was open for 24% of the time, Pallas kernels for 0%

commit v1 on v0

--- a/solution.py
+++ b/solution.py
@@ -37,7 +37,9 @@
 
 def gather_out_major(weights):
     turned = jnp.swapaxes(weights, 1, 2)
-    return lax.all_gather(turned, FSDP, axis=1, tiled=True)
+    return jnp.concatenate(
+        lax.all_to_all(jnp.stack([turned] * lax.axis_size(FSDP)), FSDP, 0, 0), axis=1
+    )
 
 
 def nt_dot(a, b):

time: 254 us -> 309 us (1.22)
  waiting for transfers between devices: 125 us -> 165 us
  local copies, waits for them, and re-layouts: 19.9 us -> 32 us
  starting transfers between devices: 11.4 us -> 21.9 us
  matrix products: 60.7 us -> 50.3 us
    all_to_all x0 -> x2, waiting for transfers between devices: none -> 117 us  [gather_out_major(): lax.all_to_all(jnp.stack([turned] * lax.axis_size(FSDP)), FSDP, 0, 0)]
    all_gather x2 -> x0, waiting for transfers between devices: 52.4 us -> none  [gather_out_major(): return lax.all_gather(turned, FSDP, axis=1, tiled=True)]
    all_gather x1, waiting for transfers between devices: 62.9 us -> 41.1 us  [per_device(): mine = lax.all_gather(own_half, BATCH, axis=0, tiled=False)]
    all_to_all x0 -> x2, starting transfers between devices: none -> 15.5 us  [gather_out_major(): lax.all_to_all(jnp.stack([turned] * lax.axis_size(FSDP)), FSDP, 0, 0)]
    dot_general x12, matrix products: 34 us -> 23.5 us  [nt_dot(): lax.dot_general(a, b, (((1,), (1,)), ((), ())), preferred_element_type=jn...]
    ppermute x1, waiting for transfers between devices: 8.15 us -> 0.01 us  [with_halo(): after = lax.ppermute(leading, axis, down)]
    ppermute x1, waiting for transfers between devices: 0.01 us -> 6.69 us  [with_halo(): before = lax.ppermute(last, axis, up)]
    ppermute x1, starting transfers between devices: 8.55 us -> 1.93 us  [with_halo(): after = lax.ppermute(leading, axis, down)]
  transfers between devices with their start and end apart: 6 -> 6, of which waited for: 3 -> 4; matrix products, arithmetic and copies ran while one was open for 24% -> 20% of each run, Pallas kernels for 0% -> 0%
where the time goes in v1:
time: 309 us; the launch traced here: 308 us
  waiting for transfers between devices  165 us (53%)
  matrix products  50.3 us (16%)
  local copies, waits for them, and re-layouts  32 us (10%)
  starting transfers between devices  21.9 us (7%)
  blocking collectives  20.7 us (7%)
  between operations  14.5 us (5%)
  other arithmetic  4.57 us (1%)
    all_to_all x2, waiting for transfers between devices, gather_out_major(): lax.all_to_all(jnp.stack([turned] * lax.axis_size(FSDP)), FSDP, 0, 0)  117 us
    all_gather x1, waiting for transfers between devices, per_device(): mine = lax.all_gather(own_half, BATCH, axis=0, tiled=False)  41.1 us
    dot_general x12, matrix products, nt_dot(): lax.dot_general(a, b, (((1,), (1,)), ((), ())), preferred_element_type=jn...  23.5 us
    all_gather x1, blocking collectives, per_device(): heads = lax.all_gather(critic_head[0], BATCH, axis=0, tiled=False)  20.7 us
    all_to_all x2, starting transfers between devices, gather_out_major(): lax.all_to_all(jnp.stack([turned] * lax.axis_size(FSDP)), FSDP, 0, 0)  15.5 us
    dot_general x1, matrix products, per_device(): jnp.einsum('gth,gch->gtc', slope_of(other, heads_other), other, preferred...  11.5 us
    dot_general x1, matrix products, per_device(): jnp.einsum('gth,gch->gtc', slope_of(mine, heads_mine), mine, preferred_el...  10.6 us
    ppermute x1, waiting for transfers between devices, with_halo(): before = lax.ppermute(last, axis, up)  6.69 us
  transfers between devices with their start and end apart: 6, of which 4 were waited for; matrix products, arithmetic and copies ran while one was open for 20% of the time, Pallas kernels for 0%

profile of v1, /device:TPU:1, one launch (start us, length us, event | category | flops | bytes accessed | tf_op | source)
XLA Modules:
  0.0 308.4 jit_solution(11979884880462471557)
XLA Ops:
  6.5 4.7 %stack.4 = bf16[16,9,40,640]{3,2,1,0:T(8,128)(2,1)} broadcast(bf16[9,40,640]{2,1,0:T(8,128)(2,1)} %bitcast.102), dimensions={1,2,3} | broadcast | bytes 7833600 | tf_op jit(solution)/shard_map/stack | solution.py:41
  11.2 10.0 %all-to-all-start = ((bf16[16,9,40,640]{3,2,1,0:T(8,128)(2,1)}), bf16[16,9,40,640]{3,2,1,0:T(8,128)(2,1)}, u32[]{:S(2)}, u32[]{:S(2)}) async-start(bf16[16,9,40,640]{3,2,1,0:T(8,128)(2,1)} %stack.4), calls=%async_computation | async-start | bytes 14745600 | tf_op jit(solution)/shard_map/all_to_all | solution.py:41
  21.3 0.2 constant_dynamic-slice_fusion.1
  21.5 1.0 copy.15
  22.5 0.2 convert_reduce_fusion.1
  22.9 0.1 reduce_sum.59
  23.2 0.4 fusion.13
  24.8 20.7 %all-gather = f32[16,1,640]{2,1,0:T(1,128)S(1)} all-gather(f32[1,1,640]{2,1,0:T(1,128)S(1)} %bitcast.104), channel_id=1, replica_groups=mesh['z'=8,'c'=2,'y'=4,'x'=4] {'y','x'}, dimensions={0}, use_global_device_ids=true | all-gather | bytes 43520 | tf_op jit(solution)/shard_map/all_gather | solution.py:60
  45.5 0.8 fusion.20
  46.3 5.3 %pad_slice_fusion = (bf16[1,32,32,640]{3,2,1,0:T(8,128)(2,1)}, bf16[1,32,32,640]{3,2,1,0:T(8,128)(2,1)}, bf16[1,32,32,640]{3,2,1,0:T(8,128)(2,1)}, bf16[1,32,32,...) fusion(bf16[1,32,32,640]{3,2,1,0:T(8,128)(2,1)S(1)} %bitcast.81), kind=kLoop, calls=%fused_computation.34 | loop fusion | bytes 11796480 | tf_op jit(solution)/shard_map/slice | solution.py:72
  51.6 41.1 %all-gather.3.cloned.1.call-done = bf16[16,640,320]{1,2,0:T(8,128)(2,1)} async-done(((bf16[1,640,320]{1,2,0:T(8,128)(2,1)}), bf16[16,640,320]{1,2,0:T(8,128)(2,1)}) %all-gather.3.cloned.1.call-update) | async-done | bytes 6553616 | tf_op jit(solution)/shard_map/all_gather | solution.py:58
  92.7 0.8 collective-permute-start.2
  93.6 89.2 %all-to-all-done = bf16[16,9,40,640]{3,2,1,0:T(8,128)(2,1)} async-done(((bf16[16,9,40,640]{3,2,1,0:T(8,128)(2,1)}), bf16[16,9,40,640]{3,2,1,0:T(8,128)(2,1)}, u32[]{:S(2)}, u32[]{:S(2)}) %all-to-all-start) | async-done | bytes 7372832 | tf_op jit(solution)/shard_map/all_to_all | solution.py:41
  182.8 1.6 stack.5
  184.4 5.6 %all-to-all-start.1 = ((bf16[16,3,40,640]{3,2,1,0:T(8,128)(2,1)}), bf16[16,3,40,640]{3,2,1,0:T(8,128)(2,1)}, u32[]{:S(2)}, u32[]{:S(2)}) async-start(bf16[16,3,40,640]{3,2,1,0:T(8,128)(2,1)} %stack.5), calls=%async_computation.1 | async-start | bytes 4915200 | tf_op jit(solution)/shard_map/all_to_all | solution.py:41
  190.0 3.9 %fusion.46 = (bf16[1,16,40,640]{3,2,0,1:T(8,128)(2,1)S(1)}, bf16[1,16,40,640]{3,2,0,1:T(8,128)(2,1)S(1)}, bf16[1,16,40,640]{3,2,0,1:T(8,128)(2,1)S(1)}, bf16[1,1...) fusion(bf16[9,16,40,640]{3,2,0,1:T(8,128)(2,1)} %bitcast.3), kind=kLoop, calls=%fused_computation.74 | loop fusion | bytes 14745600 | tf_op jit(solution)/shard_map/slice | solution.py:75
  193.9 1.3 fusion.32
  195.3 1.3 fusion.48
  196.6 1.3 fusion.49
  198.0 1.3 fusion.50
  199.3 1.3 fusion.51
  200.7 1.3 fusion.52
  202.0 1.3 fusion.53
  203.4 2.8 fusion.54
  206.2 3.5 %convert_reduce_fusion = (f32[640]{0:T(1024)S(1)}, bf16[1,1,1024,640]{3,2,1,0:T(8,128)(2,1)S(1)}) fusion(bf16[1024,640]{1,0:T(8,128)(2,1)S(1)} %bitcast.82, bf16[640,640]{1,0:T(8,128)(2,1)S(1)} %bitcast.84, f32[1024,640]{1,0:T(8,128)} %fusion.54, f32[1024,640]{1,0:T(8,128)S(1)} %fusion.53, f32[1024,640]{1,0:T(8,128)S(1)} %fusion.52, ...), kind=kOutput, calls=%fused_computation.6 | convolution fusion | flops 847379840 | bytes 25725440 | tf_op jit(solution)/shard_map/dot_general | solution.py:46
  210.2 0.4 fusion.5
  210.7 0.1 reduce_sum.84
  210.9 0.3 mul.107
  211.1 1.9 fusion.12
  213.0 3.5 %collective-permute-start = (bf16[1,1,1024,640]{3,2,1,0:T(8,128)(2,1)}, bf16[1,1,1024,640]{3,2,1,0:T(8,128)(2,1)}, u32[]{:S(2)}, u32[]{:S(2)}) collective-permute-start(bf16[1,1,1024,640]{3,2,1,0:T(8,128)(2,1)} %fusion.12), channel_id=1, source_target_pairs={{0,16},{16,32},{32,48},{48,64},{64,80},{80,96},{96,112},{112,128},... | collective-permute-start | bytes 3932168 | tf_op jit(solution)/shard_map/ppermute | solution.py:23
  216.6 0.2 select_reduce_fusion
  216.8 1.9 collective-permute-start.1
  218.7 0.2 constant_dynamic-slice_fusion.2
  218.9 27.5 %all-to-all-done.1 = bf16[16,3,40,640]{3,2,1,0:T(8,128)(2,1)} async-done(((bf16[16,3,40,640]{3,2,1,0:T(8,128)(2,1)}), bf16[16,3,40,640]{3,2,1,0:T(8,128)(2,1)}, u32[]{:S(2)}, u32[]{:S(2)}) %all-to-all-start.1) | async-done | bytes 2457632 | tf_op jit(solution)/shard_map/all_to_all | solution.py:41
  246.4 1.9 fusion.47
  248.2 2.6 fusion.28
  250.9 6.7 %collective-permute-done = bf16[1,1,1024,640]{3,2,1,0:T(8,128)(2,1)} collective-permute-done((bf16[1,1,1024,640]{3,2,1,0:T(8,128)(2,1)}, bf16[1,1,1024,640]{3,2,1,0:T(8,128)(2,1)}, u32[]{:S(2)}, u32[]{:S(2)}) %collective-permute-start) | collective-permute-done | bytes 1310752 | tf_op jit(solution)/shard_map/ppermute | solution.py:23
  257.6 2.6 fusion.30
  260.2 2.6 fusion.22
  262.8 1.7 reshape.255
  264.5 1.0 copy-done.3
  265.6 2.3 convolution_convert_fusion
  267.9 3.1 %reshape.257 = bf16[16,128,640]{2,1,0:T(8,128)(2,1)S(1)} reshape(bf16[64,20480]{1,0:T(8,128)(2,1)} %convolution_convert_fusion) | data formatting | bytes 5242880 | tf_op jit(solution)/shard_map/reshape | solution.py:100
  271.1 10.6 %fusion.23 = f32[16,128,640]{2,1,0:T(8,128)} fusion(bf16[16,640,320]{1,2,0:T(8,128)(2,1)} %all-gather.3.cloned.1.call-done, bf16[16,128,640]{2,1,0:T(8,128)(2,1)S(1)} %reshape.257, f32[16,320]{1,0:T(8,128)S(1)} %get-tuple-element.30), kind=kOutput, calls=%fused_computation.42 | convolution fusion | flops 1680343040 | bytes 14438400 | tf_op jit(solution)/shard_map/gth,gch->gtc/dot_general | solution.py:107
  281.6 11.5 %add_convert_fusion = bf16[16,128,640]{2,1,0:T(8,128)(2,1)} fusion(f32[16,128,640]{2,1,0:T(8,128)} %fusion.23, bf16[16,640,320]{1,2,0:T(8,128)(2,1)} %collective-permute-done.2, bf16[16,128,640]{2,1,0:T(8,128)(2,1)S(1)} %reshape.257, f32[16,320]{1,0:T(8,128)S(1)} %get-tuple-element.29), kind=kOutput, calls=%fused_computation.3 | convolution fusion | flops 1682964480 | bytes 17059840 | tf_op jit(solution)/shard_map/gth,gch->gtc/dot_general | solution.py:109
  293.1 4.6 %reshape.258 = bf16[64,20480]{1,0:T(8,128)(2,1)} reshape(bf16[16,128,640]{2,1,0:T(8,128)(2,1)} %add_convert_fusion) | data formatting | bytes 5242880 | tf_op jit(solution)/shard_map/reshape | solution.py:112
  297.7 2.4 fusion
  300.1 1.5 reshape.259
  (60 shorter events, 1.5 us)
Async XLA Ops:
  6.5 14.7 %copy-start = (bf16[1,640,640]{2,1,0:T(8,128)(2,1)S(1)}, bf16[1,640,640]{2,1,0:T(8,128)(2,1)}, u32[]{:S(2)}) copy-start(bf16[1,640,640]{2,1,0:T(8,128)(2,1)} %param.14) | copy-start | bytes 2457604
  11.2 171.6 %all-to-all-start = ((bf16[16,9,40,640]{3,2,1,0:T(8,128)(2,1)}), bf16[16,9,40,640]{3,2,1,0:T(8,128)(2,1)}, u32[]{:S(2)}, u32[]{:S(2)}) async-start(bf16[16,9,40,640]{3,2,1,0:T(8,128)(2,1)} %stack.4), calls=%async_computation | async-start | bytes 14745600 | tf_op jit(solution)/shard_map/all_to_all | solution.py:41
  21.2 1.3 copy-start.2
  21.2 2.8 copy-start.17
  21.2 3.6 %copy-start.16 = (f32[1,640]{1,0:T(1,128)S(1)}, f32[1,640]{1,0:T(1,128)}, u32[]{:S(2)}) copy-start(f32[1,640]{1,0:T(1,128)} %param.15) | copy-start | bytes 7684
  21.2 24.3 %copy-start.14 = (f32[640]{0:T(1024)S(1)}, f32[640]{0:T(1024)}, u32[]{:S(2)}) copy-start(f32[640]{0:T(1024)} %param.10) | copy-start | bytes 7684
  21.2 71.5 %all-gather.3.cloned.1.call-start = ((), (), s32[]{:S(2)}) async-start(), calls=%async_computation.2 | async-start | bytes 6963200 | tf_op jit(solution)/shard_map/all_gather | solution.py:58
  46.3 136.5 %copy-start.13 = (bf16[3,640,40]{1,2,0:T(8,128)(2,1)S(1)}, bf16[3,640,40]{1,2,0:T(8,128)(2,1)}, u32[]{:S(2)}) copy-start(bf16[3,640,40]{1,2,0:T(8,128)(2,1)} %param.13) | copy-start | bytes 460804
  92.7 188.9 %collective-permute-start.2 = (bf16[16,640,320]{1,2,0:T(8,128)(2,1)}, bf16[16,640,320]{1,2,0:T(8,128)(2,1)}, u32[]{:S(2)}, u32[]{:S(2)}) collective-permute-start(bf16[16,640,320]{1,2,0:T(8,128)(2,1)} %all-gather.3.cloned.1.call-done), channel_id=1, source_target_pairs={{0,16},{16,0},{1,17},{17,1},{2,18},{18,2},{3,19},{19,3},{4,20},{20... | collective-permute-start | bytes 19660808 | tf_op jit(solution)/shard_map/ppermute | solution.py:59
  184.4 62.0 %all-to-all-start.1 = ((bf16[16,3,40,640]{3,2,1,0:T(8,128)(2,1)}), bf16[16,3,40,640]{3,2,1,0:T(8,128)(2,1)}, u32[]{:S(2)}, u32[]{:S(2)}) async-start(bf16[16,3,40,640]{3,2,1,0:T(8,128)(2,1)} %stack.5), calls=%async_computation.1 | async-start | bytes 4915200 | tf_op jit(solution)/shard_map/all_to_all | solution.py:41
  193.9 1.4 copy-start.12
  195.2 1.4 copy-start.11
  196.6 1.4 copy-start.10
  198.0 1.4 copy-start.9
  199.3 1.4 copy-start.8
  200.7 1.4 copy-start.7
  202.0 1.4 copy-start.6
  203.4 2.9 copy-start.5
  206.2 4.9 %copy-start.15 = (f32[640]{0:T(1024)S(1)}, f32[640]{0:T(1024)}, u32[]{:S(2)}) copy-start(f32[640]{0:T(1024)} %param.11) | copy-start | bytes 7684
  213.0 44.5 %collective-permute-start = (bf16[1,1,1024,640]{3,2,1,0:T(8,128)(2,1)}, bf16[1,1,1024,640]{3,2,1,0:T(8,128)(2,1)}, u32[]{:S(2)}, u32[]{:S(2)}) collective-permute-start(bf16[1,1,1024,640]{3,2,1,0:T(8,128)(2,1)} %fusion.12), channel_id=1, source_target_pairs={{0,16},{16,32},{32,48},{48,64},{64,80},{80,96},{96,112},{112,128},... | collective-permute-start | bytes 3932168 | tf_op jit(solution)/shard_map/ppermute | solution.py:23
  216.8 43.5 %collective-permute-start.1 = (bf16[1,1,1024,640]{3,2,1,0:T(8,128)(2,1)}, bf16[1,1,1024,640]{3,2,1,0:T(8,128)(2,1)S(1)}, u32[]{:S(2)}, u32[]{:S(2)}) collective-permute-start(bf16[1,1,1024,640]{3,2,1,0:T(8,128)(2,1)} %fusion.12), channel_id=1, source_target_pairs={{16,0},{32,16},{48,32},{64,48},{80,64},{96,80},{112,96},{128,112},... | collective-permute-start | bytes 3932168 | tf_op jit(solution)/shard_map/ppermute | solution.py:24
  264.5 1.1 copy-start.3
  293.1 4.6 %copy-start.4 = (bf16[32,20480]{1,0:T(8,128)(2,1)S(1)}, bf16[32,20480]{1,0:T(8,128)(2,1)}, u32[]{:S(2)}) copy-start(bf16[32,20480]{1,0:T(8,128)(2,1)} %copy-done.3) | copy-start | bytes 3932164
  297.7 3.9 %copy-start.1 = (bf16[1,640,640]{2,1,0:T(8,128)(2,1)S(1)}, bf16[1,640,640]{2,1,0:T(8,128)(2,1)}, u32[]{:S(2)}) copy-start(bf16[1,640,640]{2,1,0:T(8,128)(2,1)} %param.14) | copy-start | bytes 2457604
Sparse Core Ops, SparseCore 0:
  24.5 68.2 all-gather.2
